TPU v7x, 32 devices: a whole 2x2x4 slice. The times are simulated.
32 devices in a mesh: cuts: 8 (over y, x, core), row: 4 (over z).
Axes of the slice: x: 2, y: 2, z: 4, core: 2. Of those that a mesh axis runs over, the one named last changes fastest.
Arguments:
- vectors: bfloat16 [8, 128, 98304], P('cuts', None, 'row'), may hold values from -100 to 100
- counts: int32 [8], P('cuts'), may hold values from 64 to 128, as said below
- offsets: int32 [8, 2], P('cuts'), may hold values from 0 to 96, as said below
- margin_blocks: bfloat16 [1024, 96, 288], P('row'), may hold values from -0.5 to 1.5
- energy_blocks: bfloat16 [1024, 96, 288], P('row'), may hold values from -1 to 6
- block_columns: int32 [1024, 3], P('row'), may hold values from 0 to 1023, as said below
Outputs:
- ritz_residual: bfloat16 [8, 128, 98304], P('cuts', None, 'row')
- margin_pencil: float32 [8, 128, 128], P('cuts')
- energy_pencil: float32 [8, 128, 128], P('cuts')
Inputs may be any that keep to these rules, and one draw needn't show every extreme that they name: `counts`: some slice has all 128 vectors valid and another exactly 64. offsets[s, 0] is at most 8; offsets[s, 1] + 32 lies between counts[s] - 8 and counts[s]; so both windows lie among the valid vectors. block_columns[i, 0] = i, block_columns[i, 1] lies in i - 2 to i and block_columns[i, 2] in i to i + 2.
All inputs are finite; a program needn't handle non-finite values.
Results may differ from a plain program's by a relative error of at most 0.00225.
The roundings to bfloat16 on the way count: a program that leaves them out, or rounds other values in their place, can miss the bound.
Values may be sent and summed in bfloat16 or wider, within the bound.
No kernel may reach another device: no remote copies, remote signals or barrier semaphores. Data moves between devices by JAX's collectives and lax.ppermute only.
A program may use at most 256 MiB of HBM per device.

v0:
```python
import jax
import jax.numpy as jnp
from jax import lax
from jax.sharding import PartitionSpec as P

NMAT = 98304
WIN = 32


def from_behind(block, axis, distance):
    devices = range(lax.axis_size(axis))
    route = [(i - distance, i) for i in devices if i - distance in devices]
    return lax.ppermute(block, axis, route)


def padded_2(cells, sides, width):
    for axis, dim in sides:
        count = lax.axis_size(axis)
        ends = count - 1
        head = lax.slice_in_dim(cells, 0, width, axis=dim)
        tail = lax.slice_in_dim(cells, cells.shape[dim] - width, cells.shape[dim], axis=dim)
        cells = jnp.concatenate(
            [
                lax.ppermute(tail, axis, [(i, (i + 1) % count) for i in range(ends)]),
                cells,
                lax.ppermute(head, axis, [((i + 1) % count, i) for i in range(ends)]),
            ],
            axis=dim,
        )
    return cells


def block_product(matrices, shifts, padded):
    width = padded.shape[0]
    block_rows = shifts.shape[0]
    size_block = matrices[0].shape[1]
    grid = padded.reshape(width, block_rows + 4, size_block)
    centre = grid[:, 2 : 2 + block_rows]
    choices_of = ((0,), (-2, -1, 0), (0, 1, 2))
    picked_all = []
    for column_slot in range(len(choices_of)):
        picked = centre
        for distance in choices_of[column_slot]:
            if distance != 0:
                view = grid[:, 2 + distance : 2 + distance + block_rows]
                hit = (shifts[:, column_slot] == distance)[None, :, None]
                picked = jnp.where(hit, view, picked)
        picked_all.append(picked)
    results = []
    for blocks in matrices:
        total = None
        for column_slot in range(len(choices_of)):
            part_blocks = blocks[:, :, column_slot * size_block : (column_slot + 1) * size_block]
            term = jnp.einsum(
                "cnb,nab->cna",
                picked_all[column_slot],
                part_blocks,
                preferred_element_type=jnp.float32,
            )
            total = term if total is None else total + term
        results.append(total.reshape(width, block_rows * size_block).astype(jnp.bfloat16))
    return results


def shards(vectors, counts, offsets, margin_blocks, energy_blocks, block_columns):
    own_vectors = vectors[0]
    vector_count = own_vectors.shape[0]
    block_rows = margin_blocks.shape[0]
    size_block = margin_blocks.shape[1]
    rim_width = 2 * size_block
    valid_mask = jnp.arange(vector_count, dtype=jnp.int32) < counts[0]
    masked = jnp.where(valid_mask[:, None], own_vectors, jnp.zeros((), own_vectors.dtype))
    lower_window = lax.dynamic_slice_in_dim(masked, offsets[0, 0], WIN, 0)
    upper_window = lax.dynamic_slice_in_dim(masked, offsets[0, 1], WIN, 0)
    own_blocks = lax.axis_index("row") * block_rows + jnp.arange(block_rows, dtype=jnp.int32)
    shifts = block_columns - own_blocks[:, None]
    from_below = [from_behind(upper_window, "cuts", distance) for distance in (2, 1)]
    from_above = [from_behind(lower_window, "cuts", -distance) for distance in (1, 2)]
    windows = jnp.concatenate(from_below + from_above, axis=0)
    padded_windows = padded_2(windows, (("row", 1),), rim_width)
    margin_windows = block_product((margin_blocks,), shifts, padded_windows)[0]
    partial_margin = jnp.dot(margin_windows, masked.T, preferred_element_type=jnp.float32)
    margin = lax.psum(partial_margin, "row") / NMAT
    removed = jnp.dot(margin.astype(jnp.bfloat16).T, windows, preferred_element_type=jnp.float32)
    cleaned = (masked.astype(jnp.float32) - removed).astype(jnp.bfloat16)
    padded_cleaned = padded_2(cleaned, (("row", 1),), rim_width)
    margin_cleaned, energy_cleaned = block_product(
        (margin_blocks, energy_blocks), shifts, padded_cleaned
    )
    margin_part = jnp.dot(cleaned, margin_cleaned.T, preferred_element_type=jnp.float32)
    energy_part = jnp.dot(cleaned, energy_cleaned.T, preferred_element_type=jnp.float32)
    margin_total, energy_total = lax.psum((margin_part, energy_part), "row")
    margin_pencil = margin_total / NMAT
    energy_pencil = energy_total / NMAT
    margin_diag = jnp.diagonal(margin_pencil)
    energy_diag = jnp.diagonal(energy_pencil)
    theta = jnp.where(
        valid_mask,
        energy_diag / jnp.where(valid_mask, margin_diag, jnp.float32(1.0)),
        jnp.float32(0.0),
    )
    residual = (
        energy_cleaned.astype(jnp.float32) - theta[:, None] * margin_cleaned.astype(jnp.float32)
    ).astype(jnp.bfloat16)
    return (residual[None], margin_pencil[None], energy_pencil[None])


def solution(mesh):
    placed = (
        P("cuts", None, "row"),
        P("cuts"),
        P("cuts", None),
        P("row", None, None),
        P("row", None, None),
        P("row", None),
    )
    return jax.shard_map(
        shards,
        mesh=mesh,
        in_specs=placed,
        out_specs=(P("cuts", None, "row"), P("cuts", None, None), P("cuts", None, None)),
        check_vma=False,
    )
```

profile of v0, /device:TPU:0, one launch (start us, length us, event | category | flops | bytes accessed | tf_op | source)
XLA Modules:
  0.0 498.3 jit_solution(1936045789571381187)
XLA Ops:
  32.7 10.8 %fusion.36 = (bf16[256,96,96]{0,2,1:T(8,128)(2,1)}, bf16[256,96,96]{0,2,1:T(8,128)(2,1)}, bf16[256,96,96]{0,2,1:T(8,128)(2,1)}) fusion(bf16[256,96,288]{0,2,1:T(8,128)(2,1)} %param.9), kind=kLoop, calls=%fused_computation.64 | loop fusion | bytes 28311552 | tf_op jit(solution)/shard_map/slice | solution.py:53
  43.5 17.8 %collective-permute-done = bf16[32,24576]{1,0:T(8,128)(2,1)} collective-permute-done((bf16[32,24576]{1,0:T(8,128)(2,1)}, bf16[32,24576]{1,0:T(8,128)(2,1)}, u32[]{:S(2)}, u32[]{:S(2)}) %collective-permute-start) | collective-permute-done | bytes 1572896 | tf_op jit(solution)/shard_map/ppermute | solution.py:13
  64.5 64.9 %collective-permute-done.3 = bf16[32,24576]{1,0:T(8,128)(2,1)S(1)} collective-permute-done((bf16[32,24576]{1,0:T(8,128)(2,1)}, bf16[32,24576]{1,0:T(8,128)(2,1)S(1)}, u32[]{:S(2)}, u32[]{:S(2)}) %collective-permute-start.3) | collective-permute-done | bytes 1572896 | tf_op jit(solution)/shard_map/ppermute | solution.py:13
  154.1 8.5 %copy.32 = bf16[256,96,96]{2,1,0:T(8,128)(2,1)} copy(bf16[256,96,96]{0,2,1:T(8,128)(2,1)} %get-tuple-element.12) | data formatting | bytes 9437184
  162.5 13.5 %concatenate.15 = bf16[128,24960]{1,0:T(8,128)(2,1)} concatenate(bf16[128,192]{1,0:T(8,128)(2,1)S(1)} %collective-permute-done.4, bf16[128,24576]{1,0:T(8,128)(2,1)} %copy-done.4, bf16[128,192]{1,0:T(8,128)(2,1)S(1)} %collective-permute-done.5), dimensions={1} | concatenate | bytes 12779520 | tf_op jit(solution)/shard_map/concatenate | solution.py:22
  176.0 9.2 %copy.19 = bf16[128,24960]{0,1:T(8,128)(2,1)} copy(bf16[128,24960]{1,0:T(8,128)(2,1)} %concatenate.15) | data formatting | bytes 12779520 | tf_op jit(solution)/shard_map/concatenate | solution.py:22
  185.2 11.1 %fusion.21 = f32[256,128,96]{1,2,0:T(8,128)} fusion(bf16[256,96,96]{2,1,0:T(8,128)(2,1)} %copy.30, bf16[128,260,96]{0,2,1:T(8,128)(2,1)} %bitcast.69), kind=kOutput, calls=%fused_computation.33 | convolution fusion | flops 603979776 | bytes 25165824 | tf_op jit(solution)/shard_map/cnb,nab->cna/dot_general | solution.py:54
  196.3 14.7 %fusion.8 = f32[256,128,96]{1,2,0:T(8,128)} fusion(bf16[256,96,96]{2,1,0:T(8,128)(2,1)} %copy.31, bf16[128,260,96]{0,2,1:T(8,128)(2,1)} %bitcast.70, pred[256]{0:T(512)(128)(4,1)S(1)} %get-tuple-element.4, pred[256]{0:T(512)(128)(4,1)S(1)} %get-tuple-element.6), kind=kOutput, calls=%fused_computation.18 | convolution fusion | flops 610271232 | bytes 37749248 | tf_op jit(solution)/shard_map/cnb,nab->cna/dot_general | solution.py:54
  211.1 18.4 %add_convert_fusion.2 = bf16[256,128,96]{1,2,0:T(8,128)(2,1)} fusion(f32[256,128,96]{1,2,0:T(8,128)} %fusion.21, f32[256,128,96]{1,2,0:T(8,128)} %fusion.8, bf16[256,96,96]{2,1,0:T(8,128)(2,1)S(1)} %bitcast.68, bf16[128,260,96]{0,2,1:T(8,128)(2,1)} %bitcast.71, pred[256]{0:T(512)(128)(4,1)S(1)} %get-tuple-element.5, pred[256]{0:T(512)(128)(4,1)S(1)} %get-tuple-element.3), kind=kOutput, calls=%fused_computation.7 | convolution fusion | flops 619708416 | bytes 55050752 | tf_op jit(solution)/shard_map/cnb,nab->cna/dot_general | solution.py:54
  236.9 10.8 %fusion.35 = (bf16[256,96,96]{0,2,1:T(8,128)(2,1)}, bf16[256,96,96]{0,2,1:T(8,128)(2,1)}, bf16[256,96,96]{0,2,1:T(8,128)(2,1)}) fusion(bf16[256,96,288]{0,2,1:T(8,128)(2,1)} %param.10), kind=kLoop, calls=%fused_computation.63 | loop fusion | bytes 28311552 | tf_op jit(solution)/shard_map/slice | solution.py:53
  247.7 24.5 %all-reduce.4.cloned.1.call-done = f32[128,128]{1,0:T(8,128)} async-done(((f32[128,128]{1,0:T(8,128)}), f32[128,128]{1,0:T(8,128)}) %all-reduce.4.cloned.1.call-update) | async-done | bytes 65552 | tf_op jit(solution)/shard_map/psum | solution.py:83
  302.7 8.5 %copy.34 = bf16[256,96,96]{2,1,0:T(8,128)(2,1)} copy(bf16[256,96,96]{0,2,1:T(8,128)(2,1)} %get-tuple-element.9) | data formatting | bytes 9437184
  311.2 13.5 %concatenate.16 = bf16[128,24960]{1,0:T(8,128)(2,1)} concatenate(bf16[128,192]{1,0:T(8,128)(2,1)S(1)} %collective-permute-done.6, bf16[128,24576]{1,0:T(8,128)(2,1)} %copy-done.1, bf16[128,192]{1,0:T(8,128)(2,1)S(1)} %collective-permute-done.7), dimensions={1} | concatenate | bytes 12779520 | tf_op jit(solution)/shard_map/concatenate | solution.py:22
  324.6 9.2 %copy.23 = bf16[128,24960]{0,1:T(8,128)(2,1)} copy(bf16[128,24960]{1,0:T(8,128)(2,1)} %concatenate.16) | data formatting | bytes 12779520 | tf_op jit(solution)/shard_map/concatenate | solution.py:22
  333.9 13.8 %fusion.1 = (bf16[128,256,96]{0,2,1:T(8,128)(2,1)}, bf16[128,256,96]{0,2,1:T(8,128)(2,1)S(1)}) fusion(bf16[128,260,96]{0,2,1:T(8,128)(2,1)} %bitcast.56, pred[256]{0:T(512)(128)(4,1)S(1)} %get-tuple-element.5, pred[256]{0:T(512)(128)(4,1)S(1)} %get-tuple-element.3, pred[256]{0:T(512)(128)(4,1)S(1)} %get-tuple-element.4, pred[256]{0:T(512)(128)(4,1)S(1)} %get-tuple-element.6), kind=kLoop, calls=%fused_computation.9 | loop fusion | flops 12582912 | bytes 44041216 | tf_op jit(solution)/shard_map/jit(_where)/select_n | solution.py:47
  347.7 11.4 %fusion.25 = f32[256,128,96]{1,2,0:T(8,128)} fusion(bf16[256,96,96]{2,1,0:T(8,128)(2,1)} %copy.30, bf16[128,260,96]{0,2,1:T(8,128)(2,1)S(1)} %bitcast.57), kind=kOutput, calls=%fused_computation.37 | convolution fusion | flops 603979776 | bytes 23592960 | tf_op jit(solution)/shard_map/cnb,nab->cna/dot_general | solution.py:54
  359.1 9.1 %fusion.43 = f32[256,128,96]{1,2,0:T(8,128)} fusion(bf16[256,96,96]{2,1,0:T(8,128)(2,1)} %copy.31, bf16[128,256,96]{0,2,1:T(8,128)(2,1)S(1)} %get-tuple-element.16), kind=kOutput, calls=%fused_computation.71 | convolution fusion | flops 603979776 | bytes 23592960 | tf_op jit(solution)/shard_map/cnb,nab->cna/dot_general | solution.py:54
  368.3 15.8 %add_convert_fusion = bf16[256,128,96]{1,2,0:T(8,128)(2,1)} fusion(f32[256,128,96]{1,2,0:T(8,128)} %fusion.25, f32[256,128,96]{1,2,0:T(8,128)} %fusion.43, bf16[256,96,96]{2,1,0:T(8,128)(2,1)} %copy.32, bf16[128,256,96]{0,2,1:T(8,128)(2,1)} %get-tuple-element.15), kind=kOutput, calls=%fused_computation.5 | convolution fusion | flops 613416960 | bytes 42467328 | tf_op jit(solution)/shard_map/cnb,nab->cna/dot_general | solution.py:54
  391.3 9.3 %fusion.42 = f32[256,128,96]{1,2,0:T(8,128)} fusion(bf16[256,96,96]{2,1,0:T(8,128)(2,1)} %copy.33, bf16[128,256,96]{0,2,1:T(8,128)(2,1)S(1)} %bitcast.62), kind=kOutput, calls=%fused_computation.70 | convolution fusion | flops 603979776 | bytes 23592960 | tf_op jit(solution)/shard_map/cnb,nab->cna/dot_general | solution.py:54
  400.6 9.1 %fusion.23 = f32[256,128,96]{1,2,0:T(8,128)} fusion(bf16[256,96,96]{2,1,0:T(8,128)(2,1)} %copy.29, bf16[128,260,96]{0,2,1:T(8,128)(2,1)S(1)} %bitcast.60), kind=kOutput, calls=%fused_computation.35 | convolution fusion | flops 603979776 | bytes 23592960 | tf_op jit(solution)/shard_map/cnb,nab->cna/dot_general | solution.py:54
  409.7 15.8 %add_convert_fusion.1 = bf16[256,128,96]{1,2,0:T(8,128)(2,1)} fusion(f32[256,128,96]{1,2,0:T(8,128)} %fusion.23, f32[256,128,96]{1,2,0:T(8,128)} %fusion.42, bf16[256,96,96]{2,1,0:T(8,128)(2,1)} %copy.34, bf16[128,256,96]{0,2,1:T(8,128)(2,1)} %get-tuple-element.15), kind=kOutput, calls=%fused_computation.6 | convolution fusion | flops 613416960 | bytes 42467328 | tf_op jit(solution)/shard_map/cnb,nab->cna/dot_general | solution.py:54
  447.4 12.6 %copy.27 = f32[1,128,24576]{2,1,0:T(8,128)} copy(f32[1,128,24576]{1,2,0:T(8,128)} %bitcast_convert_fusion) | data formatting | bytes 25165824 | tf_op jit(solution)/shard_map/convert_element_type | solution.py:103
  460.0 12.6 %copy.28 = f32[1,128,24576]{2,1,0:T(8,128)} copy(f32[1,128,24576]{1,2,0:T(8,128)} %bitcast_convert_fusion.1) | data formatting | bytes 25165824 | tf_op jit(solution)/shard_map/convert_element_type | solution.py:103
  479.6 11.8 %subtract_convert_fusion = bf16[1,128,24576]{2,1,0:T(8,128)(2,1)} fusion(f32[1,128,24576]{2,1,0:T(8,128)} %copy.28, f32[1,128,24576]{2,1,0:T(8,128)} %copy.27, f32[128]{0:T(128)S(1)} %divide_select_fusion), kind=kLoop, calls=%fused_computation.4 | loop fusion | flops 9437184 | bytes 31457792 | tf_op jit(solution)/shard_map/convert_element_type | solution.py:104
  (74 shorter events, 122.6 us)
Async XLA Ops:
  7.2 265.0 %all-reduce.4.cloned.1.call-start = ((), (), s32[]{:S(2)}) async-start(), calls=%async_computation | async-start | bytes 131072 | tf_op jit(solution)/shard_map/psum | solution.py:83
  16.3 2.6 copy-start.3
  18.9 13.8 %copy-start.5 = (s32[256,3]{0,1:T(4,128)S(1)}, s32[256,3]{0,1:T(4,128)}, u32[]{:S(2)}) copy-start(s32[256,3]{0,1:T(4,128)} %param.11) | copy-start | bytes 9220
  21.4 39.9 %collective-permute-start = (bf16[32,24576]{1,0:T(8,128)(2,1)}, bf16[32,24576]{1,0:T(8,128)(2,1)}, u32[]{:S(2)}, u32[]{:S(2)}) collective-permute-start(bf16[32,24576]{1,0:T(8,128)(2,1)} %get-tuple-element.22), channel_id=1, source_target_pairs={{0,8},{4,12},{8,16},{12,20},{16,24},{20,28},{1,9},{5,13},{9,17},{1... | collective-permute-start | bytes 4718600 | tf_op jit(solution)/shard_map/ppermute | solution.py:13
  27.5 35.4 %collective-permute-start.1 = (bf16[32,24576]{1,0:T(8,128)(2,1)}, bf16[32,24576]{1,0:T(8,128)(2,1)}, u32[]{:S(2)}, u32[]{:S(2)}) collective-permute-start(bf16[32,24576]{1,0:T(8,128)(2,1)} %get-tuple-element.22), channel_id=1, source_target_pairs={{0,4},{4,8},{8,12},{12,16},{16,20},{20,24},{24,28},{1,5},{5,9},{9,... | collective-permute-start | bytes 4718600 | tf_op jit(solution)/shard_map/ppermute | solution.py:13
  30.1 34.3 %collective-permute-start.2 = (bf16[32,24576]{1,0:T(8,128)(2,1)}, bf16[32,24576]{1,0:T(8,128)(2,1)S(1)}, u32[]{:S(2)}, u32[]{:S(2)}) collective-permute-start(bf16[32,24576]{1,0:T(8,128)(2,1)} %get-tuple-element.21), channel_id=1, source_target_pairs={{4,0},{8,4},{12,8},{16,12},{20,16},{24,20},{28,24},{5,1},{9,5},{13... | collective-permute-start | bytes 4718600 | tf_op jit(solution)/shard_map/ppermute | solution.py:13
  31.4 98.1 %collective-permute-start.3 = (bf16[32,24576]{1,0:T(8,128)(2,1)}, bf16[32,24576]{1,0:T(8,128)(2,1)S(1)}, u32[]{:S(2)}, u32[]{:S(2)}) collective-permute-start(bf16[32,24576]{1,0:T(8,128)(2,1)} %get-tuple-element.21), channel_id=1, source_target_pairs={{8,0},{12,4},{16,8},{20,12},{24,16},{28,20},{9,1},{13,5},{17,9},{2... | collective-permute-start | bytes 4718600 | tf_op jit(solution)/shard_map/ppermute | solution.py:13
  129.6 2.7 copy-start.4
  132.4 30.1 %collective-permute-start.4 = (bf16[128,192]{1,0:T(8,128)(2,1)S(1)}, bf16[128,192]{1,0:T(8,128)(2,1)S(1)}, u32[]{:S(2)}, u32[]{:S(2)}) collective-permute-start(bf16[128,192]{1,0:T(8,128)(2,1)S(1)} %get-tuple-element.20), channel_id=1, source_target_pairs={{0,1},{1,2},{2,3},{4,5},{5,6},{6,7},{8,9},{9,10},{10,11},{12,13},{... | collective-permute-start | bytes 147464 | tf_op jit(solution)/shard_map/ppermute | solution.py:24
  135.9 26.7 %collective-permute-start.5 = (bf16[128,192]{1,0:T(8,128)(2,1)S(1)}, bf16[128,192]{1,0:T(8,128)(2,1)S(1)}, u32[]{:S(2)}, u32[]{:S(2)}) collective-permute-start(bf16[128,192]{1,0:T(8,128)(2,1)S(1)} %get-tuple-element.19), channel_id=1, source_target_pairs={{1,0},{2,1},{3,2},{5,4},{6,5},{7,6},{9,8},{10,9},{11,10},{13,12},{... | collective-permute-start | bytes 147464 | tf_op jit(solution)/shard_map/ppermute | solution.py:26
  185.2 25.8 %slice-start.4 = ((s8[6291456]{0:T(1024)(128)(4,1)}), s8[4194304]{0:T(1024)(128)(4,1)S(1)}, s32[]{:S(2)}) async-start(s8[6291456]{0:T(1024)(128)(4,1)} %bitcast.67), calls=%async_computation.6 | async-start | bytes 8388608
  196.3 14.8 %slice-start.5 = ((s8[6291456]{0:T(1024)(128)(4,1)}), s8[2097152]{0:T(1024)(128)(4,1)S(1)}, s32[]{:S(2)}) async-start(s8[6291456]{0:T(1024)(128)(4,1)} %bitcast.67), calls=%async_computation.7 | async-start | bytes 4194304
  236.7 238.9 %all-reduce.6.cloned.1.call-start = ((), (), s32[]{:S(2)}) async-start(), calls=%async_computation.1 | async-start | bytes 262144 | tf_op jit(solution)/shard_map/psum | solution.py:92
  278.6 2.6 copy-start.1
  281.3 29.8 %collective-permute-start.6 = (bf16[128,192]{1,0:T(8,128)(2,1)S(1)}, bf16[128,192]{1,0:T(8,128)(2,1)S(1)}, u32[]{:S(2)}, u32[]{:S(2)}) collective-permute-start(bf16[128,192]{1,0:T(8,128)(2,1)S(1)} %get-tuple-element.18), channel_id=1, source_target_pairs={{0,1},{1,2},{2,3},{4,5},{5,6},{6,7},{8,9},{9,10},{10,11},{12,13},{... | collective-permute-start | bytes 147464 | tf_op jit(solution)/shard_map/ppermute | solution.py:24
  284.7 26.5 %collective-permute-start.7 = (bf16[128,192]{1,0:T(8,128)(2,1)S(1)}, bf16[128,192]{1,0:T(8,128)(2,1)S(1)}, u32[]{:S(2)}, u32[]{:S(2)}) collective-permute-start(bf16[128,192]{1,0:T(8,128)(2,1)S(1)} %get-tuple-element.17), channel_id=1, source_target_pairs={{1,0},{2,1},{3,2},{5,4},{6,5},{7,6},{9,8},{10,9},{11,10},{13,12},{... | collective-permute-start | bytes 147464 | tf_op jit(solution)/shard_map/ppermute | solution.py:26
  333.9 13.8 %copy-start = (bf16[128,24960]{0,1:T(8,128)(2,1)S(1)}, bf16[128,24960]{0,1:T(8,128)(2,1)}, u32[]{:S(2)}) copy-start(bf16[128,24960]{0,1:T(8,128)(2,1)} %copy.23) | copy-start | bytes 19169284
  347.7 11.4 %copy-start.2 = (bf16[128,256,96]{0,2,1:T(8,128)(2,1)}, bf16[128,256,96]{0,2,1:T(8,128)(2,1)S(1)}, u32[]{:S(2)}) copy-start(bf16[128,256,96]{0,2,1:T(8,128)(2,1)S(1)} %get-tuple-element.16) | copy-start | bytes 18874372
  384.1 7.2 %slice-start.2 = ((s8[6291456]{0:T(1024)(128)(4,1)}), s8[4194304]{0:T(1024)(128)(4,1)S(1)}, s32[]{:S(2)}) async-start(s8[6291456]{0:T(1024)(128)(4,1)} %bitcast.61), calls=%async_computation.4 | async-start | bytes 8388608
  384.1 7.2 %slice-start.3 = ((s8[6291456]{0:T(1024)(128)(4,1)}), s8[2097152]{0:T(1024)(128)(4,1)S(1)}, s32[]{:S(2)}) async-start(s8[6291456]{0:T(1024)(128)(4,1)} %bitcast.61), calls=%async_computation.5 | async-start | bytes 4194304
  384.1 16.5 %slice-start = ((s8[6389760]{0:T(1024)(128)(4,1)}), s8[4194304]{0:T(1024)(128)(4,1)S(1)}, s32[]{:S(2)}) async-start(s8[6389760]{0:T(1024)(128)(4,1)} %bitcast.58), calls=%async_computation.2 | async-start | bytes 8388608
  391.3 9.3 %slice-start.1 = ((s8[6389760]{0:T(1024)(128)(4,1)}), s8[2195456]{0:T(1024)(128)(4,1)S(1)}, s32[]{:S(2)}) async-start(s8[6389760]{0:T(1024)(128)(4,1)} %bitcast.58), calls=%async_computation.3 | async-start | bytes 4390912
Sparse Core Ops, SparseCore 0:
  236.8 35.3 all-reduce.3
  440.1 35.4 all-reduce.5
where the time goes:
time: 501 us; the launch traced here: 498 us
  local copies, waits for them, and re-layouts  160 us (32%)
  matrix products  143 us (29%)
  waiting for transfers between devices  110 us (22%)
  other arithmetic  45.3 us (9%)
  starting transfers between devices  20.9 us (4%)
  between operations  18.8 us (4%)
    dot_general x9, matrix products, block_product(): jnp.einsum('cnb,nab->cna', picked_all[column_slot], part_blocks, preferre...  115 us
    ppermute x4, waiting for transfers between devices, from_behind(): return lax.ppermute(block, axis, route)  82.8 us
    unnamed x33, local copies, waits for them, and re-layouts  61.5 us
    concatenate x4, local copies, waits for them, and re-layouts, padded_2(): jnp.concatenate([lax.ppermute(tail, axis, [(i, (i + 1) % count) for i in...  45.4 us
    psum x1, waiting for transfers between devices, shards(): margin = lax.psum(partial_margin, 'row') / NMAT  24.5 us
    slice x2, local copies, waits for them, and re-layouts, block_product(): blocks[:, :, column_slot * size_block:(column_slot + 1) * size_block]  21.6 us
    select_n x1, other arithmetic, block_product(): picked = jnp.where(hit, view, picked)  13.8 us
    convert_element_type x1, local copies, waits for them, and re-layouts, shards(): energy_cleaned.astype(jnp.float32)  12.6 us
  transfers between devices with their start and end apart: 10, of which 4 were waited for; matrix products, arithmetic and copies ran while one was open for 22% of the time, Pallas kernels for 0%

commit v1 on v0

--- a/solution.py
+++ b/solution.py
@@ -80,7 +80,7 @@
     padded_windows = padded_2(windows, (("row", 1),), rim_width)
     margin_windows = block_product((margin_blocks,), shifts, padded_windows)[0]
     partial_margin = jnp.dot(margin_windows, masked.T, preferred_element_type=jnp.float32)
-    margin = lax.psum(partial_margin, "row") / NMAT
+    margin = jnp.sum(lax.all_gather(partial_margin, "row"), axis=0) / NMAT
     removed = jnp.dot(margin.astype(jnp.bfloat16).T, windows, preferred_element_type=jnp.float32)
     cleaned = (masked.astype(jnp.float32) - removed).astype(jnp.bfloat16)
     padded_cleaned = padded_2(cleaned, (("row", 1),), rim_width)

time: 501 us -> 481 us (0.960)
  waiting for transfers between devices: 110 us -> 76.4 us
  blocking collectives: 0 us -> 15.5 us
    psum x1 -> x0, waiting for transfers between devices: 24.5 us -> none  [shards(): margin = lax.psum(partial_margin, 'row') / NMAT]
    all_gather x0 -> x1, blocking collectives: none -> 15.5 us  [shards(): margin = jnp.sum(lax.all_gather(partial_margin, 'row'), axis=0) / NMAT]
    ppermute x4, waiting for transfers between devices: 82.8 us -> 73.2 us  [from_behind(): return lax.ppermute(block, axis, route)]
    unnamed x33 -> x41, local copies, waits for them, and re-layouts: 61.5 us -> 65.2 us
  transfers between devices with their start and end apart: 10 -> 9, of which waited for: 4 -> 3; matrix products, arithmetic and copies ran while one was open for 22% -> 22% of each run, Pallas kernels for 0% -> 0%
where the time goes in v1:
time: 481 us; the launch traced here: 478 us
  local copies, waits for them, and re-layouts  159 us (33%)
  matrix products  142 us (30%)
  waiting for transfers between devices  76.4 us (16%)
  other arithmetic  45.2 us (9%)
  starting transfers between devices  20.7 us (4%)
  between operations  18.9 us (4%)
  blocking collectives  15.5 us (3%)
    dot_general x9, matrix products, block_product(): jnp.einsum('cnb,nab->cna', picked_all[column_slot], part_blocks, preferre...  115 us
    ppermute x4, waiting for transfers between devices, from_behind(): return lax.ppermute(block, axis, route)  73.2 us
    unnamed x41, local copies, waits for them, and re-layouts  65.2 us
    concatenate x4, local copies, waits for them, and re-layouts, padded_2(): jnp.concatenate([lax.ppermute(tail, axis, [(i, (i + 1) % count) for i in...  45.4 us
    slice x2, local copies, waits for them, and re-layouts, block_product(): blocks[:, :, column_slot * size_block:(column_slot + 1) * size_block]  17 us
    all_gather x1, blocking collectives, shards(): margin = jnp.sum(lax.all_gather(partial_margin, 'row'), axis=0) / NMAT  15.5 us
    select_n x1, other arithmetic, block_product(): picked = jnp.where(hit, view, picked)  13.8 us
    convert_element_type x1, local copies, waits for them, and re-layouts, shards(): energy_cleaned.astype(jnp.float32)  12.7 us
  transfers between devices with their start and end apart: 9, of which 3 were waited for; matrix products, arithmetic and copies ran while one was open for 22% of the time, Pallas kernels for 0%

profile of v1, /device:TPU:0, one launch (start us, length us, event | category | flops | bytes accessed | tf_op | source)
XLA Modules:
  0.0 478.2 jit_solution(10399807190659105332)
XLA Ops:
  32.8 11.9 %fusion.36 = (bf16[256,96,96]{0,2,1:T(8,128)(2,1)}, bf16[256,96,96]{0,2,1:T(8,128)(2,1)}, bf16[256,96,96]{0,2,1:T(8,128)(2,1)}) fusion(bf16[256,96,288]{0,2,1:T(8,128)(2,1)} %param.9), kind=kLoop, calls=%fused_computation.64 | loop fusion | bytes 28311552 | tf_op jit(solution)/shard_map/slice | solution.py:53
  51.8 9.6 %collective-permute-done = bf16[32,24576]{1,0:T(8,128)(2,1)} collective-permute-done((bf16[32,24576]{1,0:T(8,128)(2,1)}, bf16[32,24576]{1,0:T(8,128)(2,1)}, u32[]{:S(2)}, u32[]{:S(2)}) %collective-permute-start) | collective-permute-done | bytes 1572896 | tf_op jit(solution)/shard_map/ppermute | solution.py:13
  66.0 63.5 %collective-permute-done.3 = bf16[32,24576]{1,0:T(8,128)(2,1)S(1)} collective-permute-done((bf16[32,24576]{1,0:T(8,128)(2,1)}, bf16[32,24576]{1,0:T(8,128)(2,1)S(1)}, u32[]{:S(2)}, u32[]{:S(2)}) %collective-permute-start.3) | collective-permute-done | bytes 1572896 | tf_op jit(solution)/shard_map/ppermute | solution.py:13
  137.3 8.5 %copy.31 = bf16[256,96,96]{2,1,0:T(8,128)(2,1)} copy(bf16[256,96,96]{0,2,1:T(8,128)(2,1)} %get-tuple-element.13) | data formatting | bytes 9437184
  162.6 13.5 %concatenate.15 = bf16[128,24960]{1,0:T(8,128)(2,1)} concatenate(bf16[128,192]{1,0:T(8,128)(2,1)S(1)} %collective-permute-done.4, bf16[128,24576]{1,0:T(8,128)(2,1)} %copy-done.4, bf16[128,192]{1,0:T(8,128)(2,1)S(1)} %collective-permute-done.5), dimensions={1} | concatenate | bytes 12779520 | tf_op jit(solution)/shard_map/concatenate | solution.py:22
  176.1 9.2 %copy.19 = bf16[128,24960]{0,1:T(8,128)(2,1)} copy(bf16[128,24960]{1,0:T(8,128)(2,1)} %concatenate.15) | data formatting | bytes 12779520 | tf_op jit(solution)/shard_map/concatenate | solution.py:22
  185.3 11.0 %fusion.21 = f32[256,128,96]{1,2,0:T(8,128)} fusion(bf16[256,96,96]{2,1,0:T(8,128)(2,1)} %copy.30, bf16[128,260,96]{0,2,1:T(8,128)(2,1)} %bitcast.70), kind=kOutput, calls=%fused_computation.33 | convolution fusion | flops 603979776 | bytes 25165824 | tf_op jit(solution)/shard_map/cnb,nab->cna/dot_general | solution.py:54
  196.4 14.8 %fusion.8 = f32[256,128,96]{1,2,0:T(8,128)} fusion(bf16[256,96,96]{2,1,0:T(8,128)(2,1)} %copy.31, bf16[128,260,96]{0,2,1:T(8,128)(2,1)} %bitcast.71, pred[256]{0:T(512)(128)(4,1)S(1)} %get-tuple-element.4, pred[256]{0:T(512)(128)(4,1)S(1)} %get-tuple-element.6), kind=kOutput, calls=%fused_computation.18 | convolution fusion | flops 610271232 | bytes 37749248 | tf_op jit(solution)/shard_map/cnb,nab->cna/dot_general | solution.py:54
  211.2 18.5 %add_convert_fusion.2 = bf16[256,128,96]{1,2,0:T(8,128)(2,1)} fusion(f32[256,128,96]{1,2,0:T(8,128)} %fusion.21, f32[256,128,96]{1,2,0:T(8,128)} %fusion.8, bf16[256,96,96]{2,1,0:T(8,128)(2,1)S(1)} %bitcast.69, bf16[128,260,96]{0,2,1:T(8,128)(2,1)} %bitcast.72, pred[256]{0:T(512)(128)(4,1)S(1)} %get-tuple-element.5, pred[256]{0:T(512)(128)(4,1)S(1)} %get-tuple-element.3), kind=kOutput, calls=%fused_computation.7 | convolution fusion | flops 619708416 | bytes 55050752 | tf_op jit(solution)/shard_map/cnb,nab->cna/dot_general | solution.py:54
  236.2 15.5 %all-gather = f32[512,128]{1,0:T(8,128)S(1)} all-gather(f32[128,128]{1,0:T(8,128)S(1)} %fusion.11), channel_id=2, replica_groups=mesh['cuts'=8,'row'=4] {'row'}, dimensions={0}, use_global_device_ids=true | all-gather | bytes 327680 | tf_op jit(solution)/shard_map/all_gather | solution.py:83
  265.6 8.5 %copy.33 = bf16[256,96,96]{2,1,0:T(8,128)(2,1)} copy(bf16[256,96,96]{0,2,1:T(8,128)(2,1)} %get-tuple-element.10) | data formatting | bytes 9437184
  282.4 8.5 %copy.34 = bf16[256,96,96]{2,1,0:T(8,128)(2,1)} copy(bf16[256,96,96]{0,2,1:T(8,128)(2,1)} %get-tuple-element.9) | data formatting | bytes 9437184
  290.9 13.5 %concatenate.16 = bf16[128,24960]{1,0:T(8,128)(2,1)} concatenate(bf16[128,192]{1,0:T(8,128)(2,1)S(1)} %collective-permute-done.6, bf16[128,24576]{1,0:T(8,128)(2,1)} %copy-done.1, bf16[128,192]{1,0:T(8,128)(2,1)S(1)} %collective-permute-done.7), dimensions={1} | concatenate | bytes 12779520 | tf_op jit(solution)/shard_map/concatenate | solution.py:22
  304.4 9.2 %copy.23 = bf16[128,24960]{0,1:T(8,128)(2,1)} copy(bf16[128,24960]{1,0:T(8,128)(2,1)} %concatenate.16) | data formatting | bytes 12779520 | tf_op jit(solution)/shard_map/concatenate | solution.py:22
  313.6 13.8 %fusion.1 = (bf16[128,256,96]{0,2,1:T(8,128)(2,1)}, bf16[128,256,96]{0,2,1:T(8,128)(2,1)S(1)}) fusion(bf16[128,260,96]{0,2,1:T(8,128)(2,1)} %bitcast.57, pred[256]{0:T(512)(128)(4,1)S(1)} %get-tuple-element.5, pred[256]{0:T(512)(128)(4,1)S(1)} %get-tuple-element.3, pred[256]{0:T(512)(128)(4,1)S(1)} %get-tuple-element.4, pred[256]{0:T(512)(128)(4,1)S(1)} %get-tuple-element.6), kind=kLoop, calls=%fused_computation.9 | loop fusion | flops 12582912 | bytes 44041216 | tf_op jit(solution)/shard_map/jit(_where)/select_n | solution.py:47
  327.3 11.4 %fusion.25 = f32[256,128,96]{1,2,0:T(8,128)} fusion(bf16[256,96,96]{2,1,0:T(8,128)(2,1)} %copy.30, bf16[128,260,96]{0,2,1:T(8,128)(2,1)S(1)} %bitcast.58), kind=kOutput, calls=%fused_computation.37 | convolution fusion | flops 603979776 | bytes 23592960 | tf_op jit(solution)/shard_map/cnb,nab->cna/dot_general | solution.py:54
  338.8 9.2 %fusion.43 = f32[256,128,96]{1,2,0:T(8,128)} fusion(bf16[256,96,96]{2,1,0:T(8,128)(2,1)} %copy.31, bf16[128,256,96]{0,2,1:T(8,128)(2,1)S(1)} %get-tuple-element.16), kind=kOutput, calls=%fused_computation.71 | convolution fusion | flops 603979776 | bytes 23592960 | tf_op jit(solution)/shard_map/cnb,nab->cna/dot_general | solution.py:54
  347.9 15.8 %add_convert_fusion = bf16[256,128,96]{1,2,0:T(8,128)(2,1)} fusion(f32[256,128,96]{1,2,0:T(8,128)} %fusion.25, f32[256,128,96]{1,2,0:T(8,128)} %fusion.43, bf16[256,96,96]{2,1,0:T(8,128)(2,1)} %copy.32, bf16[128,256,96]{0,2,1:T(8,128)(2,1)} %get-tuple-element.15), kind=kOutput, calls=%fused_computation.5 | convolution fusion | flops 613416960 | bytes 42467328 | tf_op jit(solution)/shard_map/cnb,nab->cna/dot_general | solution.py:54
  370.9 9.3 %fusion.42 = f32[256,128,96]{1,2,0:T(8,128)} fusion(bf16[256,96,96]{2,1,0:T(8,128)(2,1)} %copy.33, bf16[128,256,96]{0,2,1:T(8,128)(2,1)S(1)} %bitcast.63), kind=kOutput, calls=%fused_computation.70 | convolution fusion | flops 603979776 | bytes 23592960 | tf_op jit(solution)/shard_map/cnb,nab->cna/dot_general | solution.py:54
  380.2 9.1 %fusion.23 = f32[256,128,96]{1,2,0:T(8,128)} fusion(bf16[256,96,96]{2,1,0:T(8,128)(2,1)} %copy.29, bf16[128,260,96]{0,2,1:T(8,128)(2,1)S(1)} %bitcast.61), kind=kOutput, calls=%fused_computation.35 | convolution fusion | flops 603979776 | bytes 23592960 | tf_op jit(solution)/shard_map/cnb,nab->cna/dot_general | solution.py:54
  389.3 15.8 %add_convert_fusion.1 = bf16[256,128,96]{1,2,0:T(8,128)(2,1)} fusion(f32[256,128,96]{1,2,0:T(8,128)} %fusion.23, f32[256,128,96]{1,2,0:T(8,128)} %fusion.42, bf16[256,96,96]{2,1,0:T(8,128)(2,1)} %copy.34, bf16[128,256,96]{0,2,1:T(8,128)(2,1)} %get-tuple-element.15), kind=kOutput, calls=%fused_computation.6 | convolution fusion | flops 613416960 | bytes 42467328 | tf_op jit(solution)/shard_map/cnb,nab->cna/dot_general | solution.py:54
  427.0 12.6 %copy.27 = f32[1,128,24576]{2,1,0:T(8,128)} copy(f32[1,128,24576]{1,2,0:T(8,128)} %bitcast_convert_fusion) | data formatting | bytes 25165824 | tf_op jit(solution)/shard_map/convert_element_type | solution.py:103
  439.6 12.7 %copy.28 = f32[1,128,24576]{2,1,0:T(8,128)} copy(f32[1,128,24576]{1,2,0:T(8,128)} %bitcast_convert_fusion.1) | data formatting | bytes 25165824 | tf_op jit(solution)/shard_map/convert_element_type | solution.py:103
  459.6 11.8 %subtract_convert_fusion = bf16[1,128,24576]{2,1,0:T(8,128)(2,1)} fusion(f32[1,128,24576]{2,1,0:T(8,128)} %copy.28, f32[1,128,24576]{2,1,0:T(8,128)} %copy.27, f32[128]{0:T(128)S(1)} %divide_select_fusion), kind=kLoop, calls=%fused_computation.4 | loop fusion | flops 9437184 | bytes 31457792 | tf_op jit(solution)/shard_map/convert_element_type | solution.py:104
  (82 shorter events, 122.3 us)
Async XLA Ops:
  7.2 448.4 %all-reduce.3.cloned.1.call-start = ((), (), s32[]{:S(2)}) async-start(), calls=%async_computation | async-start | bytes 262144 | tf_op jit(solution)/shard_map/psum | solution.py:92
  16.3 2.7 copy-start.3
  19.0 13.7 %copy-start.5 = (s32[256,3]{0,1:T(4,128)S(1)}, s32[256,3]{0,1:T(4,128)}, u32[]{:S(2)}) copy-start(s32[256,3]{0,1:T(4,128)} %param.11) | copy-start | bytes 9220
  19.0 25.7 %slice-start.6 = ((s8[14155776]{0:T(1024)(128)(4,1)}), s8[1572864]{0:T(1024)(128)(4,1)S(1)}, s32[]{:S(2)}) async-start(s8[14155776]{0:T(1024)(128)(4,1)} %bitcast.73), calls=%async_computation.7 | async-start | bytes 3145728
  21.5 39.9 %collective-permute-start = (bf16[32,24576]{1,0:T(8,128)(2,1)}, bf16[32,24576]{1,0:T(8,128)(2,1)}, u32[]{:S(2)}, u32[]{:S(2)}) collective-permute-start(bf16[32,24576]{1,0:T(8,128)(2,1)} %get-tuple-element.22), channel_id=1, source_target_pairs={{0,8},{4,12},{8,16},{12,20},{16,24},{20,28},{1,9},{5,13},{9,17},{1... | collective-permute-start | bytes 4718600 | tf_op jit(solution)/shard_map/ppermute | solution.py:13
  27.5 35.5 %collective-permute-start.1 = (bf16[32,24576]{1,0:T(8,128)(2,1)}, bf16[32,24576]{1,0:T(8,128)(2,1)}, u32[]{:S(2)}, u32[]{:S(2)}) collective-permute-start(bf16[32,24576]{1,0:T(8,128)(2,1)} %get-tuple-element.22), channel_id=1, source_target_pairs={{0,4},{4,8},{8,12},{12,16},{16,20},{20,24},{24,28},{1,5},{5,9},{9,... | collective-permute-start | bytes 4718600 | tf_op jit(solution)/shard_map/ppermute | solution.py:13
  30.2 34.3 %collective-permute-start.2 = (bf16[32,24576]{1,0:T(8,128)(2,1)}, bf16[32,24576]{1,0:T(8,128)(2,1)}, u32[]{:S(2)}, u32[]{:S(2)}) collective-permute-start(bf16[32,24576]{1,0:T(8,128)(2,1)} %get-tuple-element.21), channel_id=1, source_target_pairs={{4,0},{8,4},{12,8},{16,12},{20,16},{24,20},{28,24},{5,1},{9,5},{13... | collective-permute-start | bytes 4718600 | tf_op jit(solution)/shard_map/ppermute | solution.py:13
  31.5 98.1 %collective-permute-start.3 = (bf16[32,24576]{1,0:T(8,128)(2,1)}, bf16[32,24576]{1,0:T(8,128)(2,1)S(1)}, u32[]{:S(2)}, u32[]{:S(2)}) collective-permute-start(bf16[32,24576]{1,0:T(8,128)(2,1)} %get-tuple-element.21), channel_id=1, source_target_pairs={{8,0},{12,4},{16,8},{20,12},{24,16},{28,20},{9,1},{13,5},{17,9},{2... | collective-permute-start | bytes 4718600 | tf_op jit(solution)/shard_map/ppermute | solution.py:13
  32.8 11.9 %slice-start.7 = ((s8[14155776]{0:T(1024)(128)(4,1)}), s8[4194304]{0:T(1024)(128)(4,1)S(1)}, s32[]{:S(2)}) async-start(s8[14155776]{0:T(1024)(128)(4,1)} %bitcast.73), calls=%async_computation.8 | async-start | bytes 8388608
  32.8 12.1 %slice-start.8 = ((s8[14155776]{0:T(1024)(128)(4,1)}), s8[4194304]{0:T(1024)(128)(4,1)S(1)}, s32[]{:S(2)}) async-start(s8[14155776]{0:T(1024)(128)(4,1)} %bitcast.73), calls=%async_computation.9 | async-start | bytes 8388608
  32.8 13.9 %slice-start.9 = ((s8[14155776]{0:T(1024)(128)(4,1)}), s8[4194304]{0:T(1024)(128)(4,1)S(1)}, s32[]{:S(2)}) async-start(s8[14155776]{0:T(1024)(128)(4,1)} %bitcast.73), calls=%async_computation.10 | async-start | bytes 8388608
  129.7 2.7 copy-start.4
  132.5 30.2 %collective-permute-start.4 = (bf16[128,192]{1,0:T(8,128)(2,1)S(1)}, bf16[128,192]{1,0:T(8,128)(2,1)S(1)}, u32[]{:S(2)}, u32[]{:S(2)}) collective-permute-start(bf16[128,192]{1,0:T(8,128)(2,1)S(1)} %get-tuple-element.20), channel_id=1, source_target_pairs={{0,1},{1,2},{2,3},{4,5},{5,6},{6,7},{8,9},{9,10},{10,11},{12,13},{... | collective-permute-start | bytes 147464 | tf_op jit(solution)/shard_map/ppermute | solution.py:24
  136.0 26.7 %collective-permute-start.5 = (bf16[128,192]{1,0:T(8,128)(2,1)S(1)}, bf16[128,192]{1,0:T(8,128)(2,1)S(1)}, u32[]{:S(2)}, u32[]{:S(2)}) collective-permute-start(bf16[128,192]{1,0:T(8,128)(2,1)S(1)} %get-tuple-element.19), channel_id=1, source_target_pairs={{1,0},{2,1},{3,2},{5,4},{6,5},{7,6},{9,8},{10,9},{11,10},{13,12},{... | collective-permute-start | bytes 147464 | tf_op jit(solution)/shard_map/ppermute | solution.py:26
  185.3 25.8 %slice-start.4 = ((s8[6291456]{0:T(1024)(128)(4,1)}), s8[4194304]{0:T(1024)(128)(4,1)S(1)}, s32[]{:S(2)}) async-start(s8[6291456]{0:T(1024)(128)(4,1)} %bitcast.68), calls=%async_computation.5 | async-start | bytes 8388608
  196.4 14.8 %slice-start.5 = ((s8[6291456]{0:T(1024)(128)(4,1)}), s8[2097152]{0:T(1024)(128)(4,1)S(1)}, s32[]{:S(2)}) async-start(s8[6291456]{0:T(1024)(128)(4,1)} %bitcast.68), calls=%async_computation.6 | async-start | bytes 4194304
  260.9 30.0 %collective-permute-start.6 = (bf16[128,192]{1,0:T(8,128)(2,1)S(1)}, bf16[128,192]{1,0:T(8,128)(2,1)S(1)}, u32[]{:S(2)}, u32[]{:S(2)}) collective-permute-start(bf16[128,192]{1,0:T(8,128)(2,1)S(1)} %get-tuple-element.18), channel_id=1, source_target_pairs={{0,1},{1,2},{2,3},{4,5},{5,6},{6,7},{8,9},{9,10},{10,11},{12,13},{... | collective-permute-start | bytes 147464 | tf_op jit(solution)/shard_map/ppermute | solution.py:24
  264.3 26.6 %collective-permute-start.7 = (bf16[128,192]{1,0:T(8,128)(2,1)S(1)}, bf16[128,192]{1,0:T(8,128)(2,1)S(1)}, u32[]{:S(2)}, u32[]{:S(2)}) collective-permute-start(bf16[128,192]{1,0:T(8,128)(2,1)S(1)} %get-tuple-element.17), channel_id=1, source_target_pairs={{1,0},{2,1},{3,2},{5,4},{6,5},{7,6},{9,8},{10,9},{11,10},{13,12},{... | collective-permute-start | bytes 147464 | tf_op jit(solution)/shard_map/ppermute | solution.py:26
  313.6 13.8 %copy-start = (bf16[128,24960]{0,1:T(8,128)(2,1)S(1)}, bf16[128,24960]{0,1:T(8,128)(2,1)}, u32[]{:S(2)}) copy-start(bf16[128,24960]{0,1:T(8,128)(2,1)} %copy.23) | copy-start | bytes 19169284
  327.3 11.4 %copy-start.2 = (bf16[128,256,96]{0,2,1:T(8,128)(2,1)}, bf16[128,256,96]{0,2,1:T(8,128)(2,1)S(1)}, u32[]{:S(2)}) copy-start(bf16[128,256,96]{0,2,1:T(8,128)(2,1)S(1)} %get-tuple-element.16) | copy-start | bytes 18874372
  363.7 7.2 %slice-start.2 = ((s8[6291456]{0:T(1024)(128)(4,1)}), s8[4194304]{0:T(1024)(128)(4,1)S(1)}, s32[]{:S(2)}) async-start(s8[6291456]{0:T(1024)(128)(4,1)} %bitcast.62), calls=%async_computation.3 | async-start | bytes 8388608
  363.7 7.2 %slice-start.3 = ((s8[6291456]{0:T(1024)(128)(4,1)}), s8[2097152]{0:T(1024)(128)(4,1)S(1)}, s32[]{:S(2)}) async-start(s8[6291456]{0:T(1024)(128)(4,1)} %bitcast.62), calls=%async_computation.4 | async-start | bytes 4194304
  363.7 16.5 %slice-start = ((s8[6389760]{0:T(1024)(128)(4,1)}), s8[4194304]{0:T(1024)(128)(4,1)S(1)}, s32[]{:S(2)}) async-start(s8[6389760]{0:T(1024)(128)(4,1)} %bitcast.59), calls=%async_computation.1 | async-start | bytes 8388608
  370.9 9.3 %slice-start.1 = ((s8[6389760]{0:T(1024)(128)(4,1)}), s8[2195456]{0:T(1024)(128)(4,1)S(1)}, s32[]{:S(2)}) async-start(s8[6389760]{0:T(1024)(128)(4,1)} %bitcast.59), calls=%async_computation.2 | async-start | bytes 4390912
  (1 other events, 2.7 us)
Sparse Core Ops, SparseCore 0:
  419.7 35.7 all-reduce.2
